TPU v7x, 256 devices: a whole 4x4x8 slice. The times are simulated.
256 devices in a mesh: group: 32 (over z, y), tensor: 8 (over x, core).
Axes of the slice: x: 4, y: 4, z: 8, core: 2. Of those that a mesh axis runs over, the one named last changes fastest.
Arguments:
- query: bfloat16 [2, 1024, 2048], P(None, 'group', 'tensor'), may hold values from -80 to 80
- self_kv: bfloat16 [2, 1024, 2, 2048], P(None, 'group', None, 'tensor'), may hold values from -6 to 6
- kv_pages: bfloat16 [2, 1536, 16, 2, 2048], P(None, 'group', None, None, 'tensor'), may hold values from -6 to 6
- page_dest: int32 [1536, 1], replicated, may hold values from 0 to 31; in each aligned block of 48 rows (0 to 47, 48 to 95, ...) at most 3 rows name the same one
- page_request: int32 [1536], replicated, may hold values from 0 to 1
- score_len: int32 [64], P('group'), may hold values from 1 to 16
- out_proj: bfloat16 [2, 2048, 2048], P(None, 'tensor'), may hold values from -0.125 to 0.125
- residual: bfloat16 [2, 1024, 2048], P(None, ('group', 'tensor')), may hold values from -6 to 6
- norm_gain: float32 [2, 2048], replicated, may hold values from 0.5 to 40
- norm_bias: float32 [2, 2048], replicated, may hold values from -3 to 3
- vocab: bfloat16 [2, 2048, 196608], P(None, None, ('group', 'tensor')), may hold values from -0.3984375 to 0.3984375
- targets: int32 [1024], replicated, may hold values from 0 to 196607
Outputs:
- logprob: float32 [2, 1024], P(None, ('group', 'tensor'))
Inputs may be any that keep to these rules, and one draw needn't show every extreme that they name: `page_dest`: the 48 pages of each aligned block (pages held by one group) go to any one group at most 3 times; some block sends exactly 3 to some group.
All inputs are finite; a program needn't handle non-finite values.
Results may differ from a plain program's by a relative error of at most 0.00097.
Values may be sent and summed in bfloat16 or wider, within the bound.
No kernel may reach another device: no remote copies, remote signals or barrier semaphores. Data moves between devices by JAX's collectives and lax.ppermute only.
A program may use at most 128 MiB of HBM per device.

v0:
```python
import math
import jax
import jax.numpy as jnp
from jax import lax
from jax.sharding import PartitionSpec as P

HEADS = 16
HEAD_DIM = 128
REQ_GRP = 2
SCORE_LEN = 16
NEGATIVE = -1e30
EPSILON = 1e-05


def route_tables(destination, request, groups, per_owner, capacity, requests):
    page_count = destination.shape[0]
    owner_group = jnp.arange(page_count, dtype=jnp.int32) // per_owner
    columns = jnp.arange(groups, dtype=jnp.int32)
    onehot = (destination[:, None] == columns[None, :]).astype(jnp.int32)
    within = jnp.cumsum(onehot.reshape(groups, per_owner, groups), axis=1).reshape(
        page_count, groups
    )
    position = jnp.sum(within * onehot, axis=1) - 1
    arrival = owner_group * capacity + position
    combined = destination * requests + request
    pair_hot = (
        combined[:, None] == jnp.arange(groups * requests, dtype=jnp.int32)[None, :]
    ).astype(jnp.int32)
    running = jnp.cumsum(pair_hot, axis=0)
    page_rank = jnp.sum(running * pair_hot, axis=1) - 1
    totals = running[-1].reshape(groups, requests)
    return (position, arrival, page_rank, totals)


def alibi_slopes(head_count):
    return jnp.exp2(-8.0 * jnp.arange(1, head_count + 1).astype(jnp.float32) / head_count)


def per_device(
    query,
    self_kv,
    kv_pages,
    page_dest,
    page_request,
    score_len,
    out_proj,
    residual,
    norm_gain,
    norm_bias,
    vocab,
    targets,
):
    groups = lax.axis_size("group")
    shards = lax.axis_size("tensor")
    group_id = lax.axis_index("group")
    tensor_id = lax.axis_index("tensor")
    tok_grp = query.shape[1]
    flat_width = query.shape[2]
    head_local = flat_width // HEAD_DIM
    per_owner = kv_pages.shape[1]
    page_len = kv_pages.shape[2]
    capacity = 2 * per_owner // groups
    destination = page_dest[:, 0]
    page_total = destination.shape[0]
    position, arrival, page_rank, totals = route_tables(
        destination, page_request, groups, per_owner, capacity, REQ_GRP
    )
    slopes = lax.dynamic_slice_in_dim(alibi_slopes(HEADS), tensor_id * head_local, head_local)
    score_scale = 1.0 / math.sqrt(HEAD_DIM)
    queries = query.reshape(2, tok_grp, head_local, HEAD_DIM)
    own_keys = self_kv[:, :, 0].reshape(2, tok_grp, head_local, HEAD_DIM)
    own_values = self_kv[:, :, 1].reshape(2, tok_grp, head_local, HEAD_DIM)
    token_ids = jnp.arange(tok_grp, dtype=jnp.int32)
    token_request = token_ids // SCORE_LEN
    token_step = token_ids % SCORE_LEN
    own_distance = (token_step[:, None] - token_step[None, :]).astype(jnp.float32)
    own_scores = (
        jnp.einsum("mthd,mshd->mhts", queries, own_keys, preferred_element_type=jnp.float32)
        * score_scale
    )
    own_scores = own_scores - slopes[None, :, None, None] * own_distance[None, None]
    own_allowed = (
        (token_request[:, None] == token_request[None, :])
        & (token_step[None, :] <= token_step[:, None])
    )[None, None]
    own_scores = jnp.where(own_allowed, own_scores, NEGATIVE)
    own_top = jnp.max(own_scores, -1)
    my_dest = lax.dynamic_slice_in_dim(destination, group_id * per_owner, per_owner)
    my_position = lax.dynamic_slice_in_dim(position, group_id * per_owner, per_owner)
    buffer = groups * capacity
    outgoing = jnp.zeros((2, buffer, page_len, 2, flat_width), jnp.bfloat16)
    outgoing = outgoing.at[:, my_dest * capacity + my_position].set(kv_pages)
    incoming = lax.all_to_all(outgoing, "group", split_axis=1, concat_axis=1, tiled=True)
    target_place = jnp.where(destination == group_id, arrival, buffer)
    slot_index = (
        jnp.full((buffer,), page_total, jnp.int32)
        .at[target_place]
        .set(jnp.arange(page_total, dtype=jnp.int32), mode="drop")
    )
    is_valid = slot_index < page_total
    safe_index = jnp.minimum(slot_index, page_total - 1)
    key_data = incoming[:, :, :, 0].reshape(2, buffer * page_len, head_local, HEAD_DIM)
    values = incoming[:, :, :, 1].reshape(2, buffer * page_len, head_local, HEAD_DIM)
    key_request = jnp.repeat(jnp.where(is_valid, page_request[safe_index], -1), page_len)
    key_position = (
        page_rank[safe_index][:, None] * page_len + jnp.arange(page_len, dtype=jnp.int32)[None, :]
    ).reshape(-1)
    context = totals[group_id][token_request] * page_len
    distance = ((context + token_step)[:, None] - key_position[None, :]).astype(jnp.float32)
    scores = (
        jnp.einsum("mthd,mkhd->mhtk", queries, key_data, preferred_element_type=jnp.float32)
        * score_scale
    )
    scores = scores - slopes[None, :, None, None] * distance[None, None]
    allowed = (key_request[None, :] == token_request[:, None])[None, None]
    scores = jnp.where(allowed, scores, NEGATIVE)
    row_top = jnp.maximum(jnp.max(scores, -1), own_top)
    exp_terms = jnp.where(allowed, jnp.exp(scores - row_top[..., None]), 0.0)
    denominator = jnp.sum(exp_terms, -1)
    numerator = jnp.einsum(
        "mhtk,mkhd->mthd",
        exp_terms.astype(jnp.bfloat16),
        values,
        preferred_element_type=jnp.float32,
    )
    own_terms = jnp.where(own_allowed, jnp.exp(own_scores - row_top[..., None]), 0.0)
    denominator = denominator + jnp.sum(own_terms, -1)
    numerator = numerator + jnp.einsum(
        "mhts,mshd->mthd",
        own_terms.astype(jnp.bfloat16),
        own_values,
        preferred_element_type=jnp.float32,
    )
    attended = (
        (numerator / jnp.transpose(denominator, (0, 2, 1))[..., None])
        .reshape(2, tok_grp, flat_width)
        .astype(jnp.bfloat16)
    )
    rows_local = tok_grp // shards
    mixed = lax.psum_scatter(
        jnp.einsum("mtk,mkd->tmd", attended, out_proj, preferred_element_type=jnp.float32),
        "tensor",
        scatter_dimension=0,
        tiled=True,
    )
    hidden = residual.astype(jnp.float32) + jnp.transpose(mixed, (1, 0, 2))
    row_mean = jnp.mean(hidden, axis=-1, keepdims=True)
    centered = hidden - row_mean
    variance = jnp.mean(centered * centered, axis=-1, keepdims=True)
    normed = (
        centered / jnp.sqrt(variance + EPSILON) * norm_gain[:, None, :] + norm_bias[:, None, :]
    ).astype(jnp.bfloat16)
    voc_local = vocab.shape[2]
    offset = (group_id * shards + tensor_id) * voc_local
    logits = jnp.einsum(
        "mnd,mdv->mnv",
        lax.all_gather(normed, ("group", "tensor"), axis=1, tiled=True),
        vocab,
        preferred_element_type=jnp.float32,
    )
    row_peak = lax.pmax(jnp.max(logits, axis=2), ("group", "tensor"))
    wanted = targets - offset
    inside = (wanted >= 0) & (wanted < voc_local)
    picked = jnp.take_along_axis(logits, jnp.clip(wanted, 0, voc_local - 1)[None, :, None], axis=2)[
        ..., 0
    ]
    exp_total, chosen = lax.psum(
        (
            jnp.sum(jnp.exp(logits - row_peak[..., None]), axis=2),
            jnp.where(inside[None, :], picked, 0.0),
        ),
        ("group", "tensor"),
    )
    logprob_all = chosen - (row_peak + jnp.log(exp_total))
    mine = lax.dynamic_slice_in_dim(
        logprob_all, group_id * tok_grp + tensor_id * rows_local, rows_local, 1
    )
    local_ids = tensor_id * rows_local + jnp.arange(rows_local, dtype=jnp.int32)
    keep_token = local_ids % SCORE_LEN < score_len[local_ids // SCORE_LEN]
    return jnp.where(keep_token[None, :], mine, 0.0)


def solution(mesh):
    in_specs = (
        P(None, "group", "tensor"),
        P(None, "group", None, "tensor"),
        P(None, "group", None, None, "tensor"),
        P(),
        P(),
        P("group"),
        P(None, "tensor", None),
        P(None, ("group", "tensor"), None),
        P(),
        P(),
        P(None, None, ("group", "tensor")),
        P(),
    )
    out_specs = P(None, ("group", "tensor"))
    return jax.shard_map(
        per_device, mesh=mesh, in_specs=in_specs, out_specs=out_specs, check_vma=False
    )
```

profile of v0, /device:TPU:1, one launch (start us, length us, event | category | flops | bytes accessed | tf_op | source)
XLA Modules:
  0.0 520.5 jit_solution(7488796929031193324)
XLA Ops:
  6.5 0.9 reduce.1
  7.6 1.3 select_reduce_fusion
  9.0 2.9 copy.77
  12.0 2.1 broadcast_in_dim.127
  14.1 7.7 %scatter_fusion = bf16[2,96,16,2,256]{4,2,3,1,0:T(8,128)(2,1)} fusion(bf16[2,96,16,2,256]{4,2,3,1,0:T(8,128)(2,1)} %broadcast_in_dim.127, s32[48]{0:T(128)S(1)} %compare_select_fusion.5, bf16[48,2,16,2,256]{4,2,3,1,0:T(8,128)(2,1)} %copy.77), kind=kCustom, calls=%fused_computation.4 | custom fusion | bytes 4718784 | tf_op jit(solution)/shard_map/scatter | solution.py:92
  21.8 4.0 copy.78
  25.8 12.3 %all-to-all-start = ((bf16[2,96,16,2,256]{4,2,3,0,1:T(8,128)(2,1)}), bf16[2,96,16,2,256]{4,2,3,0,1:T(8,128)(2,1)}, u32[]{:S(2)}, u32[]{:S(2)}) async-start(bf16[2,96,16,2,256]{4,2,3,0,1:T(8,128)(2,1)} %copy.78), calls=%async_computation | async-start | bytes 6291456 | tf_op jit(solution)/shard_map/all_to_all | solution.py:93
  38.4 18.1 %reduce-window.6 = s32[64,12,128]{2,1,0:T(8,128)S(1)} reduce-window(s32[64,12,128]{2,1,0:T(8,128)S(1)} %fusion.29, s32[]{:T(128)} %constant.134.clone.1), window={size=1x1x128 pad=0_0x0_0x127_0}, to_apply=%region_4.5 | reduce-window | flops 12484608 | bytes 786436 | tf_op jit(solution)/shard_map/reduce-window
  56.5 0.2 slice.43
  56.8 0.3 copy.83
  57.2 0.2 broadcast_add_fusion
  57.4 0.2 select_reduce_fusion.1
  57.5 0.2 slice_reduce_fusion.2
  57.7 0.1 reshape_squeeze.17
  57.8 6.2 %scatter_custom_fusion.1 = s32[96]{0:T(128)S(1)} fusion(s32[1536]{0:T(1024)S(1)} %get-tuple-element.7, s32[1536]{0:T(1024)S(1)} %iota.68, s32[]{:T(128)} %constant.147.clone.1), kind=kCustom, calls=%fused_computation.143 | custom fusion | bytes 388 | tf_op jit(solution)/shard_map/scatter | solution.py:98
  64.0 1.1 gather_fusion.1
  65.2 1.1 gather_fusion.2
  66.8 0.6 fusion.77
  67.4 1.2 fusion.66
  68.6 0.3 slice_reduce_fusion
  69.1 0.2 fusion.79
  69.6 38.9 %all-to-all-done = bf16[2,96,16,2,256]{4,2,3,0,1:T(8,128)(2,1)} async-done(((bf16[2,96,16,2,256]{4,2,3,0,1:T(8,128)(2,1)}), bf16[2,96,16,2,256]{4,2,3,0,1:T(8,128)(2,1)}, u32[]{:S(2)}, u32[]{:S(2)}) %all-to-all-start) | async-done | bytes 3145760 | tf_op jit(solution)/shard_map/all_to_all | solution.py:93
  108.4 3.4 fusion.76
  111.8 1.3 copy.80
  113.1 3.5 reshape_squeeze.16
  116.6 2.3 fusion.78
  118.9 0.3 fusion.27
  119.2 0.2 convolution_bitcast_fusion.1
  119.4 1.3 copy.79
  120.7 3.5 reshape_squeeze.15
  124.2 1.9 fusion.22
  126.1 1.3 convolution_bitcast_fusion
  127.4 0.2 all-gather.2.cloned.1.call-start
  127.7 0.6 dynamic-slice.1
  128.9 62.4 %all-reduce.4.cloned.1.call-done = f32[32,2,2048]{2,0,1:T(8,128)} async-done(((f32[32,2,2048]{2,0,1:T(8,128)}), f32[32,2,2048]{2,0,1:T(8,128)}) %all-reduce.4.cloned.1.call-update) | async-done | bytes 524304
  191.3 1.0 fusion.58
  192.4 1.1 multiply_reduce_fusion
  193.5 1.0 add_convert_fusion
  194.5 0.6 copy.91
  195.2 0.6 gather_fusion
  195.9 119.5 %all-gather.2.cloned.1.call-done = bf16[2,1024,2048]{2,0,1:T(2,128)(2,1)} async-done(((bf16[2,4,2048]{2,0,1:T(2,128)(2,1)}), bf16[2,1024,2048]{2,0,1:T(2,128)(2,1)}) %all-gather.2.cloned.1.call-update) | async-done | bytes 8388624 | tf_op jit(solution)/shard_map/all_gather | solution.py:157
  315.4 23.1 %fusion.80 = (f32[2,1024]{1,0:T(2,128)S(1)}, f32[2,1024,768]{1,2,0:T(8,128)}) fusion(bf16[2,2048,768]{2,1,0:T(8,128)(2,1)} %param.22, bf16[2,1024,2048]{2,0,1:T(2,128)(2,1)} %all-gather.2.cloned.1.call-done), kind=kOutput, calls=%fused_computation.151 | convolution fusion | flops 6444021760 | bytes 20979712 | tf_op jit(solution)/shard_map/mnd,mdv->mnv/dot_general | solution.py:155
  338.5 10.4 %copy.94 = f32[2,1024,768]{2,0,1:T(2,128)} copy(f32[2,1024,768]{1,2,0:T(8,128)} %get-tuple-element.25) | data formatting | bytes 12582912 | tf_op jit(solution)/shard_map/mnd,mdv->mnv/dot_general | solution.py:155
  348.9 74.5 %pmax.7 = f32[2,1024]{1,0:T(2,128)S(1)} all-reduce(f32[2,1024]{1,0:T(2,128)S(1)} %get-tuple-element.24), channel_id=1, replica_groups=mesh['group'=32,'tensor'=8] {'group','tensor'}, use_global_device_ids=true, to_apply=%region_16.17 | all-reduce | flops 2048 | bytes 16384 | tf_op jit(solution)/shard_map/pmax | solution.py:161
  423.3 3.6 exponential_reduce_fusion
  427.0 12.2 %gather_fusion.3 = f32[1024,2]{0,1:T(2,128)S(1)} fusion(f32[2,1024,768]{2,0,1:T(2,128)} %copy.94, s32[1024]{0:T(1024)S(1)} %bitcast.111), kind=kCustom, calls=%fused_computation.3 | custom fusion | bytes 24576 | tf_op jit(solution)/shard_map/jit(take_along_axis)/gather | solution.py:164
  439.2 73.8 %all-reduce.1 = (f32[2,1024]{1,0:T(2,128)S(1)}, f32[2,1024]{1,0:T(2,128)S(1)}) all-reduce(f32[2,1024]{1,0:T(2,128)S(1)} %exponential_reduce_fusion, f32[2,1024]{1,0:T(2,128)S(1)} %select_bitcast_fusion), channel_id=1, replica_groups=mesh['group'=32,'tensor'=8] {'group','tensor'}, use_global_device_ids=true, to_apply=%region_18.19 | all-reduce | flops 4096 | bytes 32768 | tf_op jit(solution)/shard_map/psum | solution.py:167
  513.0 0.6 fusion.61
  (72 shorter events, 1.9 us)
Async XLA Ops:
  6.5 119.5 %copy-start = (bf16[2,256,2048]{2,1,0:T(8,128)(2,1)S(1)}, bf16[2,256,2048]{2,1,0:T(8,128)(2,1)}, u32[]{:S(2)}) copy-start(bf16[2,256,2048]{2,1,0:T(8,128)(2,1)} %param.18) | copy-start | bytes 6291460
  6.5 5.4 %copy-start.7 = (s32[1536,1]{0,1:T(1,128)S(1)}, s32[1536,1]{0,1:T(1,128)}, u32[]{:S(2)}) copy-start(s32[1536,1]{0,1:T(1,128)} %param.15) | copy-start | bytes 18436
  25.8 12.5 %copy-start.2 = (s32[1536]{0:T(1024)S(1)}, s32[1536]{0:T(1024)}, u32[]{:S(2)}) copy-start(s32[1536]{0:T(1024)} %param.16) | copy-start | bytes 18436
  25.8 82.6 %all-to-all-start = ((bf16[2,96,16,2,256]{4,2,3,0,1:T(8,128)(2,1)}), bf16[2,96,16,2,256]{4,2,3,0,1:T(8,128)(2,1)}, u32[]{:S(2)}, u32[]{:S(2)}) async-start(bf16[2,96,16,2,256]{4,2,3,0,1:T(8,128)(2,1)} %copy.78), calls=%async_computation | async-start | bytes 6291456 | tf_op jit(solution)/shard_map/all_to_all | solution.py:93
  38.1 153.2 %all-reduce.4.cloned.1.call-start = ((), (), s32[]{:S(2)}) async-start(), calls=%async_computation.2 | async-start | bytes 1048576
  56.7 11.9 %copy-start.5 = (bf16[2,32,2,256]{3,2,1,0:T(2,128)(2,1)S(1)}, bf16[2,32,2,256]{3,2,1,0:T(2,128)(2,1)}, u32[]{:S(2)}) copy-start(bf16[2,32,2,256]{3,2,1,0:T(2,128)(2,1)} %param.13) | copy-start | bytes 196612
  56.8 12.4 %copy-start.6 = (bf16[2,32,256]{2,1,0:T(8,128)(2,1)S(1)}, bf16[2,32,256]{2,1,0:T(8,128)(2,1)}, u32[]{:S(2)}) copy-start(bf16[2,32,256]{2,1,0:T(8,128)(2,1)} %param.12) | copy-start | bytes 98308
  116.6 2.8 copy-start.3
  126.0 1.6 copy-start.11
  126.1 65.3 %copy-start.4 = (bf16[2,4,2048]{2,1,0:T(4,128)(2,1)S(1)}, bf16[2,4,2048]{2,1,0:T(4,128)(2,1)}, u32[]{:S(2)}) copy-start(bf16[2,4,2048]{2,1,0:T(4,128)(2,1)} %param.19) | copy-start | bytes 98308
  126.1 67.4 %copy-start.8 = (f32[2,2048]{1,0:T(2,128)S(1)}, f32[2,2048]{1,0:T(2,128)}, u32[]{:S(2)}) copy-start(f32[2,2048]{1,0:T(2,128)} %param.21) | copy-start | bytes 49156
  126.1 67.4 %copy-start.9 = (f32[2,2048]{1,0:T(2,128)S(1)}, f32[2,2048]{1,0:T(2,128)}, u32[]{:S(2)}) copy-start(f32[2,2048]{1,0:T(2,128)} %param.20) | copy-start | bytes 49156
  126.1 69.1 %copy-start.1 = (s32[2]{0:T(128)S(1)}, s32[2]{0:T(128)}, u32[]{:S(2)}) copy-start(s32[2]{0:T(128)} %param.17) | copy-start | bytes 28
  126.1 69.7 %copy-start.10 = (s32[1024]{0:T(1024)S(1)}, s32[1024]{0:T(1024)}, u32[]{:S(2)}) copy-start(s32[1024]{0:T(1024)} %param.23) | copy-start | bytes 12292
  127.4 188.0 %all-gather.2.cloned.1.call-start = ((), (), s32[]{:S(2)}) async-start(), calls=%async_computation.1 | async-start | bytes 8421376 | tf_op jit(solution)/shard_map/all_gather | solution.py:157
Sparse Core Ops, SparseCore 0:
  127.5 63.7 all-reduce.3
  195.5 119.8 all-gather.1
where the time goes:
time: 522 us; the launch traced here: 521 us
  waiting for transfers between devices  221 us (42%)
  blocking collectives  148 us (28%)
  local copies, waits for them, and re-layouts  65 us (12%)
  other arithmetic  30.6 us (6%)
  matrix products  28.9 us (6%)
  between operations  14.5 us (3%)
  starting transfers between devices  12.5 us (2%)
    all_gather x1, waiting for transfers between devices, per_device(): lax.all_gather(normed, ('group', 'tensor'), axis=1, tiled=True)  119 us
    pmax x1, blocking collectives, per_device(): row_peak = lax.pmax(jnp.max(logits, axis=2), ('group', 'tensor'))  74.5 us
    psum x1, blocking collectives, per_device(): lax.psum((jnp.sum(jnp.exp(logits - row_peak[..., None]), axis=2), jnp.whe...  73.8 us
    unnamed x3, waiting for transfers between devices  62.5 us
    all_to_all x1, waiting for transfers between devices, per_device(): lax.all_to_all(outgoing, 'group', split_axis=1, concat_axis=1, tiled=True)  38.9 us
    dot_general x1, matrix products, per_device(): jnp.einsum('mnd,mdv->mnv', lax.all_gather(normed, ('group', 'tensor'), ax...  23.1 us
    another operation x3, other arithmetic  18.4 us
    all_to_all x1, starting transfers between devices, per_device(): lax.all_to_all(outgoing, 'group', split_axis=1, concat_axis=1, tiled=True)  12.3 us
  transfers between devices with their start and end apart: 3, of which 3 were waited for; matrix products, arithmetic and copies ran while one was open for 6% of the time, Pallas kernels for 0%

commit v1 on v0

--- a/solution.py
+++ b/solution.py
@@ -154,7 +154,12 @@
     offset = (group_id * shards + tensor_id) * voc_local
     logits = jnp.einsum(
         "mnd,mdv->mnv",
-        lax.all_gather(normed, ("group", "tensor"), axis=1, tiled=True),
+        jnp.concatenate(
+            lax.all_to_all(
+                jnp.stack([normed] * lax.axis_size(("group", "tensor"))), ("group", "tensor"), 0, 0
+            ),
+            axis=1,
+        ),
         vocab,
         preferred_element_type=jnp.float32,
     )

time: 522 us -> 620 us (1.19)
  waiting for transfers between devices: 221 us -> 286 us
  local copies, waits for them, and re-layouts: 65 us -> 92.7 us
  starting transfers between devices: 12.5 us -> 26.4 us
  matrix products: 28.9 us -> 18.7 us
    all_to_all x0 -> x1, waiting for transfers between devices: none -> 185 us  [per_device(): lax.all_to_all(jnp.stack([normed] * lax.axis_size(('group', 'tensor'))),...]
    all_gather x1 -> x0, waiting for transfers between devices: 119 us -> none  [per_device(): lax.all_gather(normed, ('group', 'tensor'), axis=1, tiled=True)]
    reshape x0 -> x2, local copies, waits for them, and re-layouts: none -> 20.9 us  [per_device(): jnp.concatenate(lax.all_to_all(jnp.stack([normed] * lax.axis_size(('group...]
    all_to_all x0 -> x1, starting transfers between devices: none -> 14.1 us  [per_device(): lax.all_to_all(jnp.stack([normed] * lax.axis_size(('group', 'tensor'))),...]
    dot_general x1, matrix products: 23.1 us -> 12.9 us  [per_device(): jnp.einsum('mnd,mdv->mnv', jnp.concatenate(lax.all_to_all(jnp.stack([norm...]
    another operation x1 -> x2, local copies, waits for them, and re-layouts: 0.1 us -> 7.59 us  [the longest x1 7.49 us: per_device(): jnp.stack([normed] * lax.axis_size(('group', 'tensor')))]
    unnamed x3 -> x2, waiting for transfers between devices: 62.5 us -> 62.6 us
  transfers between devices with their start and end apart: 3 -> 3, of which waited for: 3 -> 3; matrix products, arithmetic and copies ran while one was open for 6% -> 5% of each run, Pallas kernels for 0% -> 0%
where the time goes in v1:
time: 620 us; the launch traced here: 618 us
  waiting for transfers between devices  286 us (46%)
  blocking collectives  149 us (24%)
  local copies, waits for them, and re-layouts  92.7 us (15%)
  other arithmetic  30.6 us (5%)
  starting transfers between devices  26.4 us (4%)
  matrix products  18.7 us (3%)
  between operations  14.4 us (2%)
    all_to_all x1, waiting for transfers between devices, per_device(): lax.all_to_all(jnp.stack([normed] * lax.axis_size(('group', 'tensor'))),...  185 us
    pmax x1, blocking collectives, per_device(): row_peak = lax.pmax(jnp.max(logits, axis=2), ('group', 'tensor'))  75.5 us
    psum x1, blocking collectives, per_device(): lax.psum((jnp.sum(jnp.exp(logits - row_peak[..., None]), axis=2), jnp.whe...  73.7 us
    unnamed x2, waiting for transfers between devices  62.6 us
    all_to_all x1, waiting for transfers between devices, per_device(): lax.all_to_all(outgoing, 'group', split_axis=1, concat_axis=1, tiled=True)  38.8 us
    reshape x2, local copies, waits for them, and re-layouts, per_device(): jnp.concatenate(lax.all_to_all(jnp.stack([normed] * lax.axis_size(('group...  20.9 us
    another operation x3, other arithmetic  18.4 us
    all_to_all x1, starting transfers between devices, per_device(): lax.all_to_all(jnp.stack([normed] * lax.axis_size(('group', 'tensor'))),...  14.1 us
  transfers between devices with their start and end apart: 3, of which 3 were waited for; matrix products, arithmetic and copies ran while one was open for 5% of the time, Pallas kernels for 0%

profile of v1, /device:TPU:1, one launch (start us, length us, event | category | flops | bytes accessed | tf_op | source)
XLA Modules:
  0.0 618.1 jit_solution(5050206039626015654)
XLA Ops:
  6.5 0.9 reduce.1
  7.6 1.3 select_reduce_fusion
  9.0 2.9 copy.75
  12.0 2.1 broadcast_in_dim.127
  14.1 7.7 %scatter_fusion = bf16[2,96,16,2,256]{4,2,3,1,0:T(8,128)(2,1)} fusion(bf16[2,96,16,2,256]{4,2,3,1,0:T(8,128)(2,1)} %broadcast_in_dim.127, s32[48]{0:T(128)S(1)} %compare_select_fusion.5, bf16[48,2,16,2,256]{4,2,3,1,0:T(8,128)(2,1)} %copy.75), kind=kCustom, calls=%fused_computation.4 | custom fusion | bytes 4718784 | tf_op jit(solution)/shard_map/scatter | solution.py:92
  21.8 4.0 copy.76
  25.8 12.3 %all-to-all-start = ((bf16[2,96,16,2,256]{4,2,3,0,1:T(8,128)(2,1)}), bf16[2,96,16,2,256]{4,2,3,0,1:T(8,128)(2,1)}, u32[]{:S(2)}, u32[]{:S(2)}) async-start(bf16[2,96,16,2,256]{4,2,3,0,1:T(8,128)(2,1)} %copy.76), calls=%async_computation | async-start | bytes 6291456 | tf_op jit(solution)/shard_map/all_to_all | solution.py:93
  38.4 18.1 %reduce-window.6 = s32[64,12,128]{2,1,0:T(8,128)S(1)} reduce-window(s32[64,12,128]{2,1,0:T(8,128)S(1)} %fusion.27, s32[]{:T(128)} %constant.134.clone.1), window={size=1x1x128 pad=0_0x0_0x127_0}, to_apply=%region_4.5 | reduce-window | flops 12484608 | bytes 786436 | tf_op jit(solution)/shard_map/reduce-window
  56.6 0.2 slice.43
  56.8 0.3 copy.81
  57.2 0.2 broadcast_add_fusion
  57.5 0.2 slice_reduce_fusion.2
  57.8 6.2 scatter_custom_fusion.1
  64.0 1.1 gather_fusion.1
  65.2 1.1 gather_fusion.2
  66.8 0.6 fusion.75
  67.4 1.2 fusion.64
  68.6 0.3 slice_reduce_fusion
  69.1 0.2 fusion.77
  69.6 38.8 %all-to-all-done = bf16[2,96,16,2,256]{4,2,3,0,1:T(8,128)(2,1)} async-done(((bf16[2,96,16,2,256]{4,2,3,0,1:T(8,128)(2,1)}), bf16[2,96,16,2,256]{4,2,3,0,1:T(8,128)(2,1)}, u32[]{:S(2)}, u32[]{:S(2)}) %all-to-all-start) | async-done | bytes 3145760 | tf_op jit(solution)/shard_map/all_to_all | solution.py:93
  108.4 3.4 fusion.74
  111.8 1.3 copy.78
  113.1 3.5 reshape_squeeze.16
  116.6 2.3 fusion.76
  118.9 0.3 fusion.25
  119.2 0.2 convolution_bitcast_fusion.1
  119.4 1.3 copy.77
  120.7 3.5 reshape_squeeze.15
  124.2 1.9 fusion.20
  126.1 1.3 convolution_bitcast_fusion
  127.4 0.6 dynamic-slice.1
  128.7 62.6 %all-reduce.4.cloned.1.call-done = f32[32,2,2048]{2,0,1:T(8,128)} async-done(((f32[32,2,2048]{2,0,1:T(8,128)}), f32[32,2,2048]{2,0,1:T(8,128)}) %all-reduce.4.cloned.1.call-update) | async-done | bytes 524304
  191.3 1.0 fusion.56
  192.3 1.1 multiply_reduce_fusion
  193.4 1.0 add_convert_fusion
  194.4 7.5 %stack.2 = bf16[256,2,4,2048]{3,2,1,0:T(4,128)(2,1)} broadcast(bf16[2,4,2048]{2,1,0:T(4,128)(2,1)S(1)} %add_convert_fusion), dimensions={1,2,3} | broadcast | bytes 8421376 | tf_op jit(solution)/shard_map/stack | solution.py:159
  201.9 14.1 %all-to-all-start.1 = ((bf16[256,2,4,2048]{3,2,1,0:T(4,128)(2,1)}), bf16[256,2,4,2048]{3,2,1,0:T(4,128)(2,1)}, u32[]{:S(2)}, u32[]{:S(2)}) async-start(bf16[256,2,4,2048]{3,2,1,0:T(4,128)(2,1)} %stack.2), calls=%async_computation.1 | async-start | bytes 16777216 | tf_op jit(solution)/shard_map/all_to_all | solution.py:158
  216.1 0.6 gather_fusion
  216.8 184.7 %all-to-all-done.1 = bf16[256,2,4,2048]{3,2,1,0:T(4,128)(2,1)} async-done(((bf16[256,2,4,2048]{3,2,1,0:T(4,128)(2,1)}), bf16[256,2,4,2048]{3,2,1,0:T(4,128)(2,1)}, u32[]{:S(2)}, u32[]{:S(2)}) %all-to-all-start.1) | async-done | bytes 8388640 | tf_op jit(solution)/shard_map/all_to_all | solution.py:158
  401.5 8.4 %copy.89 = bf16[2,256,4,2048]{3,2,1,0:T(4,128)(2,1)} copy(bf16[2,256,4,2048]{3,2,0,1:T(4,128)(2,1)} %bitcast.15) | data formatting | bytes 16777216 | tf_op jit(solution)/shard_map/reshape | solution.py:157
  409.9 12.5 %reshape.499 = bf16[2,1024,2048]{2,1,0:T(8,128)(2,1)} reshape(bf16[2,256,4,2048]{3,2,1,0:T(4,128)(2,1)} %copy.89) | data formatting | bytes 16777216 | tf_op jit(solution)/shard_map/reshape | solution.py:157
  422.4 12.9 %fusion.78 = (f32[2,1024]{1,0:T(2,128)S(1)}, f32[2,1024,768]{1,2,0:T(8,128)}) fusion(bf16[2,1024,2048]{2,1,0:T(8,128)(2,1)} %reshape.499, bf16[2,2048,768]{2,1,0:T(8,128)(2,1)} %param.22), kind=kOutput, calls=%fused_computation.149 | convolution fusion | flops 6444021760 | bytes 20979712 | tf_op jit(solution)/shard_map/mnd,mdv->mnv/dot_general | solution.py:155
  435.3 10.3 %copy.91 = f32[2,1024,768]{2,0,1:T(2,128)} copy(f32[2,1024,768]{1,2,0:T(8,128)} %get-tuple-element.25) | data formatting | bytes 12582912 | tf_op jit(solution)/shard_map/mnd,mdv->mnv/dot_general | solution.py:155
  445.6 75.5 %pmax.7 = f32[2,1024]{1,0:T(2,128)S(1)} all-reduce(f32[2,1024]{1,0:T(2,128)S(1)} %get-tuple-element.24), channel_id=1, replica_groups=mesh['group'=32,'tensor'=8] {'group','tensor'}, use_global_device_ids=true, to_apply=%region_16.17 | all-reduce | flops 2048 | bytes 16384 | tf_op jit(solution)/shard_map/pmax | solution.py:166
  521.1 3.6 exponential_reduce_fusion
  524.7 12.2 %gather_fusion.3 = f32[1024,2]{0,1:T(2,128)S(1)} fusion(f32[2,1024,768]{2,0,1:T(2,128)} %copy.91, s32[1024]{0:T(1024)S(1)} %bitcast.113), kind=kCustom, calls=%fused_computation.3 | custom fusion | bytes 24576 | tf_op jit(solution)/shard_map/jit(take_along_axis)/gather | solution.py:169
  537.0 73.7 %all-reduce.1 = (f32[2,1024]{1,0:T(2,128)S(1)}, f32[2,1024]{1,0:T(2,128)S(1)}) all-reduce(f32[2,1024]{1,0:T(2,128)S(1)} %exponential_reduce_fusion, f32[2,1024]{1,0:T(2,128)S(1)} %select_bitcast_fusion), channel_id=1, replica_groups=mesh['group'=32,'tensor'=8] {'group','tensor'}, use_global_device_ids=true, to_apply=%region_18.19 | all-reduce | flops 4096 | bytes 32768 | tf_op jit(solution)/shard_map/psum | solution.py:172
  610.6 0.6 fusion.59
  (75 shorter events, 2.2 us)
Async XLA Ops:
  6.5 119.6 %copy-start = (bf16[2,256,2048]{2,1,0:T(8,128)(2,1)S(1)}, bf16[2,256,2048]{2,1,0:T(8,128)(2,1)}, u32[]{:S(2)}) copy-start(bf16[2,256,2048]{2,1,0:T(8,128)(2,1)} %param.18) | copy-start | bytes 6291460
  6.5 5.4 copy-start.8
  25.8 12.5 %copy-start.3 = (s32[1536]{0:T(1024)S(1)}, s32[1536]{0:T(1024)}, u32[]{:S(2)}) copy-start(s32[1536]{0:T(1024)} %param.16) | copy-start | bytes 18436
  25.8 82.6 %all-to-all-start = ((bf16[2,96,16,2,256]{4,2,3,0,1:T(8,128)(2,1)}), bf16[2,96,16,2,256]{4,2,3,0,1:T(8,128)(2,1)}, u32[]{:S(2)}, u32[]{:S(2)}) async-start(bf16[2,96,16,2,256]{4,2,3,0,1:T(8,128)(2,1)} %copy.76), calls=%async_computation | async-start | bytes 6291456 | tf_op jit(solution)/shard_map/all_to_all | solution.py:93
  38.1 153.1 %all-reduce.4.cloned.1.call-start = ((), (), s32[]{:S(2)}) async-start(), calls=%async_computation.2 | async-start | bytes 1048576
  38.4 30.2 %copy-start.6 = (bf16[2,32,2,256]{3,2,1,0:T(2,128)(2,1)S(1)}, bf16[2,32,2,256]{3,2,1,0:T(2,128)(2,1)}, u32[]{:S(2)}) copy-start(bf16[2,32,2,256]{3,2,1,0:T(2,128)(2,1)} %param.13) | copy-start | bytes 196612
  38.4 30.7 %copy-start.7 = (bf16[2,32,256]{2,1,0:T(8,128)(2,1)S(1)}, bf16[2,32,256]{2,1,0:T(8,128)(2,1)}, u32[]{:S(2)}) copy-start(bf16[2,32,256]{2,1,0:T(8,128)(2,1)} %param.12) | copy-start | bytes 98308
  116.6 2.8 copy-start.4
  124.2 3.3 copy-start.12
  124.2 67.1 %copy-start.5 = (bf16[2,4,2048]{2,1,0:T(4,128)(2,1)S(1)}, bf16[2,4,2048]{2,1,0:T(4,128)(2,1)}, u32[]{:S(2)}) copy-start(bf16[2,4,2048]{2,1,0:T(4,128)(2,1)} %param.19) | copy-start | bytes 98308
  124.2 69.2 %copy-start.9 = (f32[2,2048]{1,0:T(2,128)S(1)}, f32[2,2048]{1,0:T(2,128)}, u32[]{:S(2)}) copy-start(f32[2,2048]{1,0:T(2,128)} %param.21) | copy-start | bytes 49156
  124.2 69.2 %copy-start.10 = (f32[2,2048]{1,0:T(2,128)S(1)}, f32[2,2048]{1,0:T(2,128)}, u32[]{:S(2)}) copy-start(f32[2,2048]{1,0:T(2,128)} %param.20) | copy-start | bytes 49156
  201.9 14.1 %copy-start.2 = (s32[2]{0:T(128)S(1)}, s32[2]{0:T(128)}, u32[]{:S(2)}) copy-start(s32[2]{0:T(128)} %param.17) | copy-start | bytes 28
  201.9 14.8 %copy-start.11 = (s32[1024]{0:T(1024)S(1)}, s32[1024]{0:T(1024)}, u32[]{:S(2)}) copy-start(s32[1024]{0:T(1024)} %param.23) | copy-start | bytes 12292
  201.9 199.6 %all-to-all-start.1 = ((bf16[256,2,4,2048]{3,2,1,0:T(4,128)(2,1)}), bf16[256,2,4,2048]{3,2,1,0:T(4,128)(2,1)}, u32[]{:S(2)}, u32[]{:S(2)}) async-start(bf16[256,2,4,2048]{3,2,1,0:T(4,128)(2,1)} %stack.2), calls=%async_computation.1 | async-start | bytes 16777216 | tf_op jit(solution)/shard_map/all_to_all | solution.py:158
  445.6 165.6 %copy-start.1 = (bf16[2,256,2048]{2,1,0:T(8,128)(2,1)S(1)}, bf16[2,256,2048]{2,1,0:T(8,128)(2,1)}, u32[]{:S(2)}) copy-start(bf16[2,256,2048]{2,1,0:T(8,128)(2,1)} %param.18) | copy-start | bytes 6291460
Sparse Core Ops, SparseCore 0:
  127.5 63.6 all-reduce.3
